TPU v7x, 512 devices: a whole 4x8x8 slice. The times are simulated.
512 devices in a mesh: seq: 64 (over y, x, core), ch: 8 (over z).
Axes of the slice: x: 4, y: 8, z: 8, core: 2. Of those that a mesh axis runs over, the one named last changes fastest.
Arguments:
- signal: bfloat16 [1536, 32768], P('ch', 'seq'), may hold values from -16 to 16
- input_norm_gain: float32 [1536], P('ch'), may hold values from 0.25 to 1.75
- value_weight: bfloat16 [1536, 1536], P('seq', 'ch'), may hold values from -0.15625 to 0.15625
- gate_weight: bfloat16 [1536, 1536], P('seq', 'ch'), may hold values from -0.15625 to 0.15625
- depth_taps: float32 [31, 1536], P(None, 'ch'), may hold values from -1 to 1
- cotangent: bfloat16 [1536, 32768], P('ch', 'seq'), may hold values from -6 to 6
Outputs:
- output: bfloat16 [1536, 32768], P('ch', 'seq')
- signal_gradient: bfloat16 [1536, 32768], P('ch', 'seq')
- grad_value: float32 [1536, 1536], P('seq', 'ch')
- grad_gate: float32 [1536, 1536], P('seq', 'ch')
- grad_taps: float32 [31, 1536], P(None, 'ch')
- gain_gradient: float32 [1536], P('ch')
All inputs are finite; a program needn't handle non-finite values.
Results may differ from a plain program's by a relative error of at most 0.02.
Values may be sent and summed in bfloat16 or wider, within the bound.
No kernel may reach another device: no remote copies, remote signals or barrier semaphores. Data moves between devices by JAX's collectives and lax.ppermute only.
A program may use at most 64 MiB of HBM per device.

v0:
```python
import jax
import jax.numpy as jnp
from jax import lax
from jax.sharding import PartitionSpec as P


def extended(cells, sides, width):
    for axis, dim in sides:
        count = lax.axis_size(axis)
        ends = count - 1
        head = lax.slice_in_dim(cells, 0, width, axis=dim)
        tail = lax.slice_in_dim(cells, cells.shape[dim] - width, cells.shape[dim], axis=dim)
        cells = jnp.concatenate(
            [
                lax.ppermute(tail, axis, [(i, (i + 1) % count) for i in range(ends)]),
                cells,
                lax.ppermute(head, axis, [((i + 1) % count, i) for i in range(ends)]),
            ],
            axis=dim,
        )
    return cells


def standardize_rows(columns_in):
    values = columns_in.astype(jnp.float32)
    average = jnp.mean(values, 0, keepdims=True)
    centred = values - average
    spread = jnp.mean(centred * centred, 0, keepdims=True)
    inverse_deviation = lax.rsqrt(spread + 1e-05)
    return (centred * inverse_deviation, inverse_deviation)


def depthwise(padded, kernel):
    channels = padded.shape[0]
    result = lax.conv_general_dilated(
        padded[None],
        kernel,
        (1,),
        "VALID",
        dimension_numbers=("NCH", "OIH", "NCH"),
        feature_group_count=channels,
        precision=lax.Precision.HIGHEST,
    )
    return result[0]


def shards(signal, input_norm_gain, value_weight, gate_weight, depth_taps, cotangent):
    local_cols = signal.shape[0]
    frames = signal.shape[1]
    groups = lax.axis_size("ch")
    block_of_rows = frames // groups
    channel_position = lax.axis_index("ch")
    reach = depth_taps.shape[0] // 2
    complete_signal, complete_gain = (
        lax.all_gather(signal, "ch", axis=0, tiled=True),
        lax.all_gather(input_norm_gain.astype(jnp.bfloat16), "ch", axis=0, tiled=True).astype(
            input_norm_gain.dtype
        ),
    )
    centered_unit, inverse_deviation = standardize_rows(complete_signal)
    normalized_signal = (centered_unit * complete_gain[:, None]).astype(jnp.bfloat16)
    centered_unit_rows = lax.dynamic_slice_in_dim(
        centered_unit, channel_position * block_of_rows, block_of_rows, 1
    )
    row_inverse_deviation = lax.dynamic_slice_in_dim(
        inverse_deviation, channel_position * block_of_rows, block_of_rows, 1
    )
    stacked = jnp.concatenate([value_weight, gate_weight], 1)
    gathered = lax.all_gather(stacked, "seq", axis=0, tiled=True)
    mixed = lax.dot_general(
        gathered, normalized_signal, (((0,), (0,)), ((), ())), preferred_element_type=jnp.float32
    )
    value = mixed[:local_cols]
    gate = mixed[local_cols:]
    sig_gate = jax.nn.sigmoid(gate)
    glued = (value * sig_gate).astype(jnp.bfloat16)
    glued_pad = extended(glued, (("seq", 1),), reach).astype(jnp.float32)
    forward_kernel = depth_taps.T[:, None, :]
    pre = depthwise(glued_pad, forward_kernel)
    sig_pre = jax.nn.sigmoid(pre)
    output = (pre * sig_pre).astype(jnp.bfloat16)
    grad_pre = (cotangent.astype(jnp.float32) * sig_pre * (1.0 + pre * (1.0 - sig_pre))).astype(
        jnp.bfloat16
    )
    grad_pre_f = grad_pre.astype(jnp.float32)
    grad_pad = extended(grad_pre, (("seq", 1),), reach).astype(jnp.float32)
    grad_glued = depthwise(grad_pad, forward_kernel[:, :, ::-1])
    tap_partial = depthwise(glued_pad, grad_pre_f[:, None, :]).T
    grad_taps = lax.psum(tap_partial, "seq")
    grad_v = (grad_glued * sig_gate).astype(jnp.bfloat16)
    grad_g = (grad_glued * value * sig_gate * (1.0 - sig_gate)).astype(jnp.bfloat16)
    grad_both = jnp.concatenate([grad_v, grad_g], 0)
    weight_sums = lax.psum_scatter(
        lax.dot_general(
            normalized_signal,
            grad_both,
            (((1,), (1,)), ((), ())),
            preferred_element_type=jnp.float32,
        ),
        "seq",
        scatter_dimension=0,
        tiled=True,
    )
    grad_value = weight_sums[:, :local_cols]
    grad_gate = weight_sums[:, local_cols:]
    normed_term = jnp.dot(gathered, grad_both, preferred_element_type=jnp.float32)
    normalized_gradient = lax.psum_scatter(
        normed_term.astype(jnp.bfloat16), "ch", scatter_dimension=1, tiled=True
    ).astype(jnp.float32)
    scaled_signal = normalized_gradient * complete_gain[:, None]
    first_moment = jnp.mean(scaled_signal, 0, keepdims=True)
    second_moment = jnp.mean(scaled_signal * centered_unit_rows, 0, keepdims=True)
    gradient_rows = (
        row_inverse_deviation * (scaled_signal - first_moment - centered_unit_rows * second_moment)
    ).astype(jnp.bfloat16)
    signal_gradient = lax.all_to_all(gradient_rows, "ch", split_axis=0, concat_axis=1, tiled=True)
    gain_portion = jnp.sum(normalized_gradient * centered_unit_rows, 1)
    gain_whole = lax.psum(gain_portion, ("seq", "ch"))
    gain_gradient = lax.dynamic_slice_in_dim(
        gain_whole, channel_position * local_cols, local_cols, 0
    )
    return (output, signal_gradient, grad_value, grad_gate, grad_taps, gain_gradient)


def solution(mesh):
    placed = (
        P("ch", "seq"),
        P("ch"),
        P("seq", "ch"),
        P("seq", "ch"),
        P(None, "ch"),
        P("ch", "seq"),
    )
    return jax.shard_map(
        shards,
        mesh=mesh,
        in_specs=placed,
        out_specs=(
            P("ch", "seq"),
            P("ch", "seq"),
            P("seq", "ch"),
            P("seq", "ch"),
            P(None, "ch"),
            P("ch"),
        ),
        check_vma=False,
    )
```

profile of v0, /device:TPU:1, one launch (start us, length us, event | category | flops | bytes accessed | tf_op | source)
XLA Modules:
  0.0 592.0 jit_solution(6644750311934210366)
XLA Ops:
  8.0 1.4 pad_maximum_fusion.4
  10.1 1.3 dynamic-slice.4
  12.3 20.2 %all-reduce = bf16[1536]{0:T(1024)(128)(2,1)S(1)} all-reduce(bf16[1536]{0:T(1024)(128)(2,1)S(1)} %dynamic-update-slice), channel_id=1, replica_groups=mesh['seq'=64,'ch'=8] {'ch'}, use_global_device_ids=true, to_apply=%add | all-reduce | flops 1536 | bytes 6144
  32.6 22.6 %all-gather.5.cloned.1.call-done = bf16[1536,512]{1,0:T(8,128)(2,1)} async-done(((bf16[192,512]{1,0:T(8,128)(2,1)}), bf16[1536,512]{1,0:T(8,128)(2,1)}) %all-gather.5.cloned.1.call-update) | async-done | bytes 1572880 | tf_op jit(solution)/shard_map/all_gather | solution.py:55
  55.2 1.7 copy.41
  57.8 85.3 %all-gather.3.cloned.1.call-done = bf16[1536,384]{1,0:T(8,128)(2,1)} async-done(((bf16[24,384]{1,0:T(8,128)(2,1)}), bf16[1536,384]{1,0:T(8,128)(2,1)}) %all-gather.3.cloned.1.call-update) | async-done | bytes 1179664 | tf_op jit(solution)/shard_map/all_gather | solution.py:69
  143.1 2.2 fusion.6
  145.6 2.1 collective-permute-start.1
  147.7 3.4 collective-permute-start
  151.2 1.1 collective-permute-done
  154.1 2.0 convolution_select_fusion.1
  156.1 1.4 copy.58
  158.5 2.0 multiply_convert_fusion.5
  160.6 1.9 collective-permute-start.3
  162.5 4.2 collective-permute-start.2
  166.8 1.1 collective-permute-done.2
  168.9 2.0 convolution_select_fusion
  171.0 1.4 copy.59
  172.4 1.0 reshape.81
  173.4 1.2 multiply_convert_fusion.4
  174.6 3.5 convolution_convert_fusion
  178.4 1.3 dynamic-slice.5
  180.4 2.1 fusion
  183.8 2.7 fusion.5
  186.5 38.9 %reduce-scatter.2.cloned.1.call-done = bf16[1536,64]{0,1:T(8,128)(2,1)} async-done(((bf16[1536,512]{0,1:T(8,128)(2,1)}), bf16[1536,64]{0,1:T(8,128)(2,1)}) %reduce-scatter.2.cloned.1.call-update) | async-done | bytes 196624 | tf_op jit(solution)/shard_map/reduce_scatter | solution.py:107
  225.4 1.3 fusion.26
  226.7 1.2 fusion.24
  228.9 4.7 all-to-all-start
  233.6 2.2 fusion.49
  235.9 245.9 %psum.14 = f32[31,192]{1,0:T(8,128)} all-reduce(f32[31,192]{1,0:T(8,128)S(1)} %bitcast.60), channel_id=1, replica_groups=mesh['seq'=64,'ch'=8] {'seq'}, use_global_device_ids=true, to_apply=%region_6.0 | all-reduce | flops 5952 | bytes 47616 | tf_op jit(solution)/shard_map/psum | solution.py:89
  481.8 1.5 fusion.46
  483.3 100.8 %psum.15 = f32[1536]{0:T(1024)S(1)} all-reduce(f32[1536]{0:T(1024)S(1)} %get-tuple-element.18), channel_id=1, replica_groups=mesh['seq'=64,'ch'=8] {'seq','ch'}, use_global_device_ids=true, to_apply=%region_8.0 | all-reduce | flops 1536 | bytes 12288 | tf_op jit(solution)/shard_map/psum | solution.py:118
  (49 shorter events, 10.7 us)
Async XLA Ops:
  7.2 146.9 %copy-start = (f32[31,192]{1,0:T(8,128)S(1)}, f32[31,192]{1,0:T(8,128)}, u32[]{:S(2)}) copy-start(f32[31,192]{1,0:T(8,128)} %param.10) | copy-start | bytes 71428
  7.2 48.0 %all-gather.5.cloned.1.call-start = ((), (), s32[]{:S(2)}) async-start(), calls=%async_computation.3 | async-start | bytes 1769472 | tf_op jit(solution)/shard_map/all_gather | solution.py:55
  7.9 135.2 %all-gather.3.cloned.1.call-start = ((), (), s32[]{:S(2)}) async-start(), calls=%async_computation.2 | async-start | bytes 1198080 | tf_op jit(solution)/shard_map/all_gather | solution.py:69
  9.4 216.0 %reduce-scatter.2.cloned.1.call-start = ((), (), s32[]{:S(2)}) async-start(), calls=%async_computation.4 | async-start | bytes 1769472 | tf_op jit(solution)/shard_map/reduce_scatter | solution.py:107
  145.3 8.7 %copy-start.2 = (pred[8,68]{0,1:T(8,128)(4,1)S(1)}, pred[8,68]{0,1:T(8,128)(4,1)}, u32[]{:S(2)}) copy-start(pred[8,68]{0,1:T(8,128)(4,1)} %constant.43) | copy-start | bytes 1636
  145.6 5.6 collective-permute-start.1
  147.7 4.6 collective-permute-start
  160.6 6.2 %collective-permute-start.3 = (bf16[192,15]{1,0:T(8,128)(2,1)S(1)}, bf16[192,15]{1,0:T(8,128)(2,1)S(1)}, u32[]{:S(2)}, u32[]{:S(2)}) collective-permute-start(bf16[192,15]{1,0:T(8,128)(2,1)S(1)} %get-tuple-element.30), channel_id=1, source_target_pairs={{8,0},{16,8},{24,16},{32,24},{40,32},{48,40},{56,48},{64,56},{72,6... | collective-permute-start | bytes 17288 | tf_op jit(solution)/shard_map/ppermute | solution.py:17
  162.5 5.4 collective-permute-start.2
  178.1 4.3 copy-start.1
  178.1 303.6 %all-reduce.4.cloned.1.call-start = ((), (), s32[]{:S(2)}) async-start(), calls=%async_computation.5 | async-start | bytes 4718592
  228.9 355.8 %all-to-all-start = ((bf16[8,192,64]{1,2,0:T(8,128)(2,1)}), bf16[8,192,64]{1,2,0:T(8,128)(2,1)S(1)}, u32[]{:S(2)}, u32[]{:S(2)}) async-start(bf16[8,192,64]{1,2,0:T(8,128)(2,1)} %copy.54), calls=%async_computation.1 | async-start | bytes 524288 | tf_op jit(solution)/shard_map/all_to_all | solution.py:116
Sparse Core Ops, SparseCore 0:
  10.1 45.0 all-gather.4
  59.0 84.0 all-gather.2
  178.3 47.0 reduce-scatter.1
  228.6 202.0 all-reduce.3
where the time goes:
time: 593 us; the launch traced here: 592 us
  blocking collectives  367 us (62%)
  waiting for transfers between devices  150 us (25%)
  starting transfers between devices  16.8 us (3%)
  local copies, waits for them, and re-layouts  16.6 us (3%)
  between operations  15.3 us (3%)
  matrix products  14.7 us (2%)
  other arithmetic  11.8 us (2%)
    psum x1, blocking collectives, shards(): grad_taps = lax.psum(tap_partial, 'seq')  246 us
    psum x1, blocking collectives, shards(): gain_whole = lax.psum(gain_portion, ('seq', 'ch'))  101 us
    all_gather x1, waiting for transfers between devices, shards(): gathered = lax.all_gather(stacked, 'seq', axis=0, tiled=True)  85.3 us
    reduce_scatter x1, waiting for transfers between devices, shards(): lax.psum_scatter(normed_term.astype(jnp.bfloat16), 'ch', scatter_dimensio...  38.9 us
    all_gather x1, waiting for transfers between devices, shards(): lax.all_gather(signal, 'ch', axis=0, tiled=True)  22.6 us
    unnamed x1, blocking collectives  20.2 us
  transfers between devices with their start and end apart: 9, of which 5 were waited for; matrix products, arithmetic and copies ran while one was open for 4% of the time, Pallas kernels for 0%

commit v1 on v0

--- a/solution.py
+++ b/solution.py
@@ -2,6 +2,22 @@
 import jax.numpy as jnp
 from jax import lax
 from jax.sharding import PartitionSpec as P
+
+
+def spread_the_targets(array_here):
+    ndev = lax.axis_size("ch")
+    rows = [(u, (u + 1) % ndev) for u in range(ndev)]
+    table = [(u, (u - 1) % ndev) for u in range(ndev)]
+    last, side_arr = ([array_here], [array_here])
+    for _ in range(ndev // 2):
+        spare = lax.ppermute(last[-1], "ch", rows)
+        last.append(spare)
+    for _ in range((ndev - 1) // 2):
+        local_now = lax.ppermute(side_arr[-1], "ch", perm=table)
+        side_arr.append(local_now)
+    val2 = jnp.concatenate([*last[::-1], *side_arr[1:]], 0)
+    piece_now = lax.axis_index("ch")
+    return jnp.roll(val2, (piece_now - ndev // 2) * array_here.shape[0], 0)
 
 
 def extended(cells, sides, width):
@@ -52,7 +68,7 @@
     channel_position = lax.axis_index("ch")
     reach = depth_taps.shape[0] // 2
     complete_signal, complete_gain = (
-        lax.all_gather(signal, "ch", axis=0, tiled=True),
+        spread_the_targets(signal),
         lax.all_gather(input_norm_gain.astype(jnp.bfloat16), "ch", axis=0, tiled=True).astype(
             input_norm_gain.dtype
         ),

time: 593 us -> 564 us (0.951)
  waiting for transfers between devices: 150 us -> 72.6 us
  starting transfers between devices: 16.8 us -> 45 us
  local copies, waits for them, and re-layouts: 16.6 us -> 36.5 us
  blocking collectives: 367 us -> 360 us
    all_gather x1, waiting for transfers between devices: 85.3 us -> 26.2 us  [shards(): gathered = lax.all_gather(stacked, 'seq', axis=0, tiled=True)]
    ppermute x0 -> x7, starting transfers between devices: none -> 28.3 us  [the longest x3 17.7 us: spread_the_targets(): local_now = lax.ppermute(side_arr[-1], 'ch', perm=table)]
    all_gather x1 -> x0, waiting for transfers between devices: 22.6 us -> none  [shards(): lax.all_gather(signal, 'ch', axis=0, tiled=True)]
    conv_general_dilated x10, local copies, waits for them, and re-layouts: 6.57 us -> 16.6 us  [depthwise(): lax.conv_general_dilated(padded[None], kernel, (1,), 'VALID', dimension_n...]
    ppermute x0 -> x7, waiting for transfers between devices: none -> 9.45 us  [the longest x4 9.44 us: spread_the_targets(): spare = lax.ppermute(last[-1], 'ch', rows)]
    unnamed x1, blocking collectives: 20.2 us -> 13.6 us
  transfers between devices with their start and end apart: 9 -> 15, of which waited for: 5 -> 7; matrix products, arithmetic and copies ran while one was open for 4% -> 6% of each run, Pallas kernels for 0% -> 0%
where the time goes in v1:
time: 564 us; the launch traced here: 562 us
  blocking collectives  360 us (64%)
  waiting for transfers between devices  72.6 us (13%)
  starting transfers between devices  45 us (8%)
  local copies, waits for them, and re-layouts  36.5 us (6%)
  matrix products  18 us (3%)
  between operations  15.5 us (3%)
  other arithmetic  14.7 us (3%)
    psum x1, blocking collectives, shards(): grad_taps = lax.psum(tap_partial, 'seq')  246 us
    psum x1, blocking collectives, shards(): gain_whole = lax.psum(gain_portion, ('seq', 'ch'))  101 us
    reduce_scatter x1, waiting for transfers between devices, shards(): lax.psum_scatter(normed_term.astype(jnp.bfloat16), 'ch', scatter_dimensio...  34.8 us
    all_gather x1, waiting for transfers between devices, shards(): gathered = lax.all_gather(stacked, 'seq', axis=0, tiled=True)  26.2 us
    ppermute x3, starting transfers between devices, spread_the_targets(): local_now = lax.ppermute(side_arr[-1], 'ch', perm=table)  17.7 us
    conv_general_dilated x10, local copies, waits for them, and re-layouts, depthwise(): lax.conv_general_dilated(padded[None], kernel, (1,), 'VALID', dimension_n...  16.6 us
    unnamed x1, blocking collectives  13.6 us
  transfers between devices with their start and end apart: 15, of which 7 were waited for; matrix products, arithmetic and copies ran while one was open for 6% of the time, Pallas kernels for 0%

profile of v1, /device:TPU:1, one launch (start us, length us, event | category | flops | bytes accessed | tf_op | source)
XLA Modules:
  0.0 562.3 jit_solution(11069177538668482787)
XLA Ops:
  9.8 4.8 collective-permute-start
  14.6 8.6 %collective-permute-start.4 = (bf16[192,512]{0,1:T(8,128)(2,1)S(1)}, bf16[192,512]{0,1:T(8,128)(2,1)S(1)}, u32[]{:S(2)}, u32[]{:S(2)}) collective-permute-start(bf16[192,512]{0,1:T(8,128)(2,1)S(1)} %copy.47), channel_id=1, source_target_pairs={{0,7},{1,0},{2,1},{3,2},{4,3},{5,4},{6,5},{7,6},{8,15},{9,8},{10,9... | collective-permute-start | bytes 589832 | tf_op jit(solution)/shard_map/ppermute | solution.py:16
  23.2 4.1 collective-permute-done
  29.2 4.6 collective-permute-start.5
  33.8 3.1 collective-permute-done.1
  38.9 4.6 collective-permute-start.6
  43.5 2.2 collective-permute-done.2
  50.5 13.6 %all-reduce = bf16[1536]{0:T(1024)(128)(2,1)S(1)} all-reduce(bf16[1536]{0:T(1024)(128)(2,1)S(1)} %dynamic-update-slice), channel_id=1, replica_groups=mesh['seq'=64,'ch'=8] {'ch'}, use_global_device_ids=true, to_apply=%add | all-reduce | flops 1536 | bytes 6144
  64.9 5.5 concatenate.19
  73.2 26.2 %all-gather.2.cloned.1.call-done = bf16[1536,384]{1,0:T(8,128)(2,1)} async-done(((bf16[24,384]{1,0:T(8,128)(2,1)}), bf16[1536,384]{1,0:T(8,128)(2,1)}) %all-gather.2.cloned.1.call-update) | async-done | bytes 1179664 | tf_op jit(solution)/shard_map/all_gather | solution.py:85
  99.4 2.9 fusion.6
  103.4 2.1 collective-permute-start.8
  105.5 3.4 collective-permute-start.7
  113.6 2.0 convolution_select_fusion.1
  115.7 2.3 copy.67
  117.9 2.2 reshape.80
  120.1 2.0 multiply_convert_fusion.5
  124.1 4.4 collective-permute-start.9
  130.4 2.1 reshape.84
  132.4 2.1 copy.59
  135.5 3.0 convolution_select_fusion
  138.5 2.3 copy.68
  140.8 2.2 reshape.81
  145.1 3.6 convolution_convert_fusion
  150.7 2.9 fusion
  153.6 2.1 copy.64
  156.8 4.3 fusion.5
  161.1 34.8 %reduce-scatter.2.cloned.1.call-done = bf16[1536,64]{0,1:T(8,128)(2,1)} async-done(((bf16[1536,512]{0,1:T(8,128)(2,1)}), bf16[1536,64]{0,1:T(8,128)(2,1)}) %reduce-scatter.2.cloned.1.call-update) | async-done | bytes 196624 | tf_op jit(solution)/shard_map/reduce_scatter | solution.py:123
  199.5 4.7 all-to-all-start
  204.2 2.2 fusion.49
  206.4 245.8 %psum.14 = f32[31,192]{1,0:T(8,128)} all-reduce(f32[31,192]{1,0:T(8,128)S(1)} %bitcast.60), channel_id=1, replica_groups=mesh['seq'=64,'ch'=8] {'seq'}, use_global_device_ids=true, to_apply=%region_6.7 | all-reduce | flops 5952 | bytes 47616 | tf_op jit(solution)/shard_map/psum | solution.py:105
  453.7 100.6 %psum.15 = f32[1536]{0:T(1024)S(1)} all-reduce(f32[1536]{0:T(1024)S(1)} %get-tuple-element.18), channel_id=1, replica_groups=mesh['seq'=64,'ch'=8] {'seq','ch'}, use_global_device_ids=true, to_apply=%region_8.9 | all-reduce | flops 1536 | bytes 12288 | tf_op jit(solution)/shard_map/psum | solution.py:134
  (81 shorter events, 35.6 us)
Async XLA Ops:
  7.2 106.4 %copy-start = (f32[31,192]{1,0:T(8,128)S(1)}, f32[31,192]{1,0:T(8,128)}, u32[]{:S(2)}) copy-start(f32[31,192]{1,0:T(8,128)} %param.10) | copy-start | bytes 71428
  7.2 92.2 %all-gather.2.cloned.1.call-start = ((), (), s32[]{:S(2)}) async-start(), calls=%async_computation.2 | async-start | bytes 1198080 | tf_op jit(solution)/shard_map/all_gather | solution.py:85
  8.7 187.2 %reduce-scatter.2.cloned.1.call-start = ((), (), s32[]{:S(2)}) async-start(), calls=%async_computation.3 | async-start | bytes 1769472 | tf_op jit(solution)/shard_map/reduce_scatter | solution.py:123
  9.8 17.5 %collective-permute-start = (bf16[192,512]{0,1:T(8,128)(2,1)S(1)}, bf16[192,512]{0,1:T(8,128)(2,1)S(1)}, u32[]{:S(2)}, u32[]{:S(2)}) collective-permute-start(bf16[192,512]{0,1:T(8,128)(2,1)S(1)} %copy.47), channel_id=1, source_target_pairs={{0,1},{1,2},{2,3},{3,4},{4,5},{5,6},{6,7},{7,0},{8,9},{9,10},{10,1... | collective-permute-start | bytes 589832 | tf_op jit(solution)/shard_map/ppermute | solution.py:13
  14.6 14.6 %collective-permute-start.4 = (bf16[192,512]{0,1:T(8,128)(2,1)S(1)}, bf16[192,512]{0,1:T(8,128)(2,1)S(1)}, u32[]{:S(2)}, u32[]{:S(2)}) collective-permute-start(bf16[192,512]{0,1:T(8,128)(2,1)S(1)} %copy.47), channel_id=1, source_target_pairs={{0,7},{1,0},{2,1},{3,2},{4,3},{5,4},{6,5},{7,6},{8,15},{9,8},{10,9... | collective-permute-start | bytes 589832 | tf_op jit(solution)/shard_map/ppermute | solution.py:16
  27.3 1.9 copy-start.2
  27.3 9.7 %collective-permute-start.1 = (bf16[192,512]{0,1:T(8,128)(2,1)S(1)}, bf16[192,512]{0,1:T(8,128)(2,1)S(1)}, u32[]{:S(2)}, u32[]{:S(2)}) collective-permute-start(bf16[192,512]{0,1:T(8,128)(2,1)S(1)} %collective-permute-done), channel_id=1, source_target_pairs={{0,1},{1,2},{2,3},{3,4},{4,5},{5,6},{6,7},{7,0},{8,9},{9,10},{10,1... | collective-permute-start | bytes 589832 | tf_op jit(solution)/shard_map/ppermute | solution.py:13
  29.2 7.7 %copy-start.3 = (bf16[192,512]{0,1:T(8,128)(2,1)}, bf16[192,512]{0,1:T(8,128)(2,1)S(1)}, u32[]{:S(2)}) copy-start(bf16[192,512]{0,1:T(8,128)(2,1)S(1)} %collective-permute-done.4) | copy-start | bytes 589828
  29.2 9.6 %collective-permute-start.5 = (bf16[192,512]{0,1:T(8,128)(2,1)S(1)}, bf16[192,512]{0,1:T(8,128)(2,1)S(1)}, u32[]{:S(2)}, u32[]{:S(2)}) collective-permute-start(bf16[192,512]{0,1:T(8,128)(2,1)S(1)} %collective-permute-done.4), channel_id=1, source_target_pairs={{0,7},{1,0},{2,1},{3,2},{4,3},{5,4},{6,5},{7,6},{8,15},{9,8},{10,9... | collective-permute-start | bytes 589832 | tf_op jit(solution)/shard_map/ppermute | solution.py:16
  37.0 1.9 copy-start.4
  37.0 8.7 %collective-permute-start.2 = (bf16[192,512]{0,1:T(8,128)(2,1)S(1)}, bf16[192,512]{0,1:T(8,128)(2,1)S(1)}, u32[]{:S(2)}, u32[]{:S(2)}) collective-permute-start(bf16[192,512]{0,1:T(8,128)(2,1)S(1)} %collective-permute-done.1), channel_id=1, source_target_pairs={{0,1},{1,2},{2,3},{3,4},{4,5},{5,6},{6,7},{7,0},{8,9},{9,10},{10,1... | collective-permute-start | bytes 589832 | tf_op jit(solution)/shard_map/ppermute | solution.py:13
  38.9 25.3 %copy-start.5 = (bf16[192,512]{0,1:T(8,128)(2,1)}, bf16[192,512]{0,1:T(8,128)(2,1)S(1)}, u32[]{:S(2)}) copy-start(bf16[192,512]{0,1:T(8,128)(2,1)S(1)} %collective-permute-done.5) | copy-start | bytes 589828
  38.9 25.3 %collective-permute-start.6 = (bf16[192,512]{0,1:T(8,128)(2,1)S(1)}, bf16[192,512]{0,1:T(8,128)(2,1)S(1)}, u32[]{:S(2)}, u32[]{:S(2)}) collective-permute-start(bf16[192,512]{0,1:T(8,128)(2,1)S(1)} %collective-permute-done.5), channel_id=1, source_target_pairs={{0,7},{1,0},{2,1},{3,2},{4,3},{5,4},{6,5},{7,6},{8,15},{9,8},{10,9... | collective-permute-start | bytes 589832 | tf_op jit(solution)/shard_map/ppermute | solution.py:16
  45.7 18.5 %copy-start.6 = (bf16[192,512]{0,1:T(8,128)(2,1)}, bf16[192,512]{0,1:T(8,128)(2,1)S(1)}, u32[]{:S(2)}) copy-start(bf16[192,512]{0,1:T(8,128)(2,1)S(1)} %collective-permute-done.2) | copy-start | bytes 589828
  45.7 19.2 %collective-permute-start.3 = (bf16[192,512]{0,1:T(8,128)(2,1)S(1)}, bf16[192,512]{0,1:T(8,128)(2,1)}, u32[]{:S(2)}, u32[]{:S(2)}) collective-permute-start(bf16[192,512]{0,1:T(8,128)(2,1)S(1)} %collective-permute-done.2), channel_id=1, source_target_pairs={{0,1},{1,2},{2,3},{3,4},{4,5},{5,6},{6,7},{7,0},{8,9},{9,10},{10,1... | collective-permute-start | bytes 589832 | tf_op jit(solution)/shard_map/ppermute | solution.py:13
  64.2 0.7 copy-start.7
  102.3 0.9 copy-start.1
  103.2 10.4 %copy-start.12 = (pred[8,68]{0,1:T(8,128)(4,1)S(1)}, pred[8,68]{0,1:T(8,128)(4,1)}, u32[]{:S(2)}) copy-start(pred[8,68]{0,1:T(8,128)(4,1)} %constant.63) | copy-start | bytes 1636
  103.4 5.6 collective-permute-start.8
  105.5 4.6 collective-permute-start.7
  122.1 6.4 %collective-permute-start.10 = (bf16[192,15]{1,0:T(8,128)(2,1)S(1)}, bf16[192,15]{1,0:T(8,128)(2,1)S(1)}, u32[]{:S(2)}, u32[]{:S(2)}) collective-permute-start(bf16[192,15]{1,0:T(8,128)(2,1)S(1)} %get-tuple-element.30), channel_id=1, source_target_pairs={{8,0},{16,8},{24,16},{32,24},{40,32},{48,40},{56,48},{64,56},{72,6... | collective-permute-start | bytes 17288 | tf_op jit(solution)/shard_map/ppermute | solution.py:33
  124.1 5.4 collective-permute-start.9
  144.3 0.7 copy-start.8
  144.3 0.7 copy-start.9
  148.7 303.6 %all-reduce.4.cloned.1.call-start = ((), (), s32[]{:S(2)}) async-start(), calls=%async_computation.4 | async-start | bytes 4718592
  161.1 43.0 %copy-start.10 = (bf16[1,192,542]{1,0,2:T(2,128)(2,1)S(1)}, bf16[1,192,542]{1,0,2:T(2,128)(2,1)}, u32[]{:S(2)}) copy-start(bf16[1,192,542]{1,0,2:T(2,128)(2,1)} %copy.64) | copy-start | bytes 624388
  161.1 43.0 %copy-start.11 = (bf16[192,1,512]{0,1,2:T(2,128)(2,1)S(1)}, bf16[192,1,512]{0,1,2:T(2,128)(2,1)}, u32[]{:S(2)}) copy-start(bf16[192,1,512]{0,1,2:T(2,128)(2,1)} %copy.65) | copy-start | bytes 589828
  199.5 355.5 %all-to-all-start = ((bf16[8,192,64]{1,2,0:T(8,128)(2,1)}), bf16[8,192,64]{1,2,0:T(8,128)(2,1)S(1)}, u32[]{:S(2)}, u32[]{:S(2)}) async-start(bf16[8,192,64]{1,2,0:T(8,128)(2,1)} %copy.63), calls=%async_computation.1 | async-start | bytes 524288 | tf_op jit(solution)/shard_map/all_to_all | solution.py:132
Sparse Core Ops, SparseCore 0:
  11.9 87.4 all-gather.1
  148.8 47.0 reduce-scatter.1
  199.3 202.0 all-reduce.3
